TPU v7x, 32 devices: a whole 2x2x4 slice. The times are simulated.
32 devices in a mesh: groups: 2 (over y), seq: 4 (over z), head: 2 (over x), cfg: 2 (over core).
Axes of the slice: x: 2, y: 2, z: 4, core: 2. Of those that a mesh axis runs over, the one named last changes fastest.
Arguments:
- q_img: bfloat16 [2, 4096, 1536], P('cfg', ('groups', 'seq'), 'head'), parts along dimension 1
- k_img: bfloat16 [2, 4096, 1536], P('cfg', ('groups', 'seq'), 'head'), parts along dimension 1
- v_img: bfloat16 [2, 4096, 1536], P('cfg', ('groups', 'seq'), 'head'), parts along dimension 1, may hold values from -6 to 6
- text_keys: bfloat16 [2, 8, 333, 1536], P('cfg', 'groups', None, 'head'), parts along dimension 1
- text_values: bfloat16 [2, 8, 333, 1536], P('cfg', 'groups', None, 'head'), parts along dimension 1, may hold values from -6 to 6
- text_lengths: int32 [2, 8], P('cfg', 'groups'), parts along dimension 1, may hold values from 1 to 333, as said below
- img_lengths: int32 [8], P('groups'), parts along dimension 0, may hold values from 1 to 1024, 2048 in all
- out_weight: bfloat16 [1536, 2432], P(None, 'head'), may hold values from -0.15625 to 0.15625
Outputs:
- guided: bfloat16 [4096, 2432], P(('groups', 'seq'), ('head', 'cfg')), parts along dimension 0
There are 2 independent parts, one for each index of `groups`. A program takes and returns all parts, laid end to end along the dimension named above; an argument that names none is the same for every part. Nothing has to cross between parts.
Inputs may be any that keep to these rules, and one draw needn't show every extreme that they name: `img_lengths`: request r holds the image positions from the sum of the earlier lengths on; the lengths sum to 2048. text_lengths[b, r] of request r's 333 text slots are live in branch b, the first ones.
All inputs are finite; a program needn't handle non-finite values.
Results may differ from a plain program's by a relative error of at most 0.009.
Values may be sent and summed in bfloat16 or wider, within the bound.
No kernel may reach another device: no remote copies, remote signals or barrier semaphores. Data moves between devices by JAX's collectives and lax.ppermute only.
A program may use at most 128 MiB of HBM per device.

v0:
```python
import functools

import jax
import jax.numpy as jnp
from jax import lax
from jax.experimental import pallas as pl
from jax.experimental.pallas import tpu as pltpu
from jax.sharding import PartitionSpec as P

HDIM = 64


guidance = 4.0
score_scale = 0.125
neg_large = -1e30


def partner_2(x, axis, distance):
    return lax.ppermute(x, axis, [(i, i ^ 1 << distance) for i in range(lax.axis_size(axis))])


def seg_scalar(info_ref, pos, reqs):
    seg = jnp.int32(0)
    for r in range(reqs):
        seg = seg + jnp.where(pos >= info_ref[2 + r], 1, 0).astype(jnp.int32)
    return seg


def seg_vector(info_ref, pos, reqs):
    seg = jnp.zeros(pos.shape, jnp.int32)
    for r in range(reqs):
        seg = seg + (pos >= info_ref[2 + r]).astype(jnp.int32)
    return seg


def attn_kernel(info_ref, q_ref, k_ref, v_ref, *refs, kind, heads, reqs, tq, tk, total, first, last, sub):
    if first:
        ins, outs = (), refs[:-3]
    else:
        ins, outs = refs[:3], refs[3:-3]
    m_sc, l_sc, a_sc = refs[-3:]
    qi = pl.program_id(0)
    b = pl.program_id(1)
    nb = pl.num_programs(1)
    width = heads * HDIM

    @pl.when(b == 0)
    def _():
        if first:
            m_sc[...] = jnp.full(m_sc.shape, neg_large, jnp.float32)
            l_sc[...] = jnp.zeros(l_sc.shape, jnp.float32)
            a_sc[...] = jnp.zeros(a_sc.shape, jnp.float32)
        else:
            m_sc[...] = ins[0][...]
            l_sc[...] = ins[1][...]
            a_sc[...] = ins[2][...]

    qpos0 = info_ref[0] + qi * tq
    qlo = seg_scalar(info_ref, qpos0, reqs)
    qhi = seg_scalar(info_ref, qpos0 + tq - 1, reqs)
    if kind == "text":
        req = b // sub
        offset = (b % sub) * tk
        active = (qlo <= req) & (req <= qhi) & (offset < info_ref[2 + reqs + req])
    else:
        kpos0 = info_ref[1] + b * tk
        klo = seg_scalar(info_ref, kpos0, reqs)
        khi = seg_scalar(info_ref, kpos0 + tk - 1, reqs)
        active = (kpos0 >= 0) & (kpos0 < total) & (klo <= qhi) & (qlo <= khi)

    @pl.when(active)
    def _():
        qseg = seg_vector(info_ref, qpos0 + lax.broadcasted_iota(jnp.int32, (1, tq), 1), reqs)
        row = lax.broadcasted_iota(jnp.int32, (tk, 1), 0)
        if kind == "text":
            mask = (row + offset < info_ref[2 + reqs + req]) & (qseg == req)
        else:
            mask = seg_vector(info_ref, kpos0 + row, reqs) == qseg
        for g0 in range(0, width, 128):
            gw = min(128, width - g0)
            qg = q_ref[:, g0:g0 + gw]
            kg = k_ref[0, :, g0:g0 + gw]
            vt = v_ref[0, :, g0:g0 + gw].T
            lane = lax.broadcasted_iota(jnp.int32, (1, gw), 1)
            sub = lax.broadcasted_iota(jnp.int32, (gw, 1), 0) < HDIM
            acc = a_sc[g0:g0 + gw, :]
            parts = []
            for i in range(gw // HDIM):
                h = g0 // HDIM + i
                if gw == HDIM:
                    kh = kg
                else:
                    kh = jnp.where((lane < HDIM) if i == 0 else (lane >= HDIM), kg, jnp.zeros_like(kg))
                st = lax.dot_general(
                    kh, qg, (((1,), (1,)), ((), ())), preferred_element_type=jnp.float32
                ) * score_scale
                st = jnp.where(mask, st, neg_large)
                m_old = m_sc[h]
                m_new = jnp.maximum(m_old, jnp.max(st, axis=0, keepdims=True))
                alpha = jnp.exp(m_old - m_new)
                pt = jnp.exp(st - m_new)
                l_sc[h] = alpha * l_sc[h] + jnp.sum(pt, axis=0, keepdims=True)
                m_sc[h] = m_new
                pv = jnp.dot(vt, pt.astype(jnp.bfloat16), preferred_element_type=jnp.float32)
                parts.append(alpha * acc + pv)
            new = parts[0] if len(parts) == 1 else jnp.where(sub, parts[0], parts[1])
            a_sc[g0:g0 + gw, :] = new

    @pl.when(b == nb - 1)
    def _():
        if last:
            for g0 in range(0, width, 128):
                gw = min(128, width - g0)
                h = g0 // HDIM
                if gw == HDIM:
                    den = l_sc[h]
                else:
                    sub = lax.broadcasted_iota(jnp.int32, (gw, 1), 0) < HDIM
                    den = jnp.where(sub, l_sc[h], l_sc[h + 1])
                outs[0][g0:g0 + gw, :] = (a_sc[g0:g0 + gw, :] / den).astype(outs[0].dtype)
        else:
            outs[0][...] = m_sc[...]
            outs[1][...] = l_sc[...]
            outs[2][...] = a_sc[...]


def attend_chunk(info, queries, keys, values, v_off, state, *, kind, reqs, total, last, part=(0, 1), tq=256, sub=1):
    tok, full_width = queries.shape
    index, nparts = part
    width = full_width // nparts
    heads = width // HDIM
    nb = keys.shape[0] - v_off
    tk = keys.shape[1]
    tq = min(tok, tq)
    first = state is None
    kernel = functools.partial(
        attn_kernel, kind=kind, heads=heads, reqs=reqs, tq=tq, tk=tk, total=total, first=first, last=last, sub=sub
    )
    q_spec = pl.BlockSpec((tq, width), lambda qi, b, info: (qi, index))
    k_spec = pl.BlockSpec((1, tk, width), lambda qi, b, info: (b, 0, index))
    v_spec = pl.BlockSpec((1, tk, width), lambda qi, b, info: (v_off + b, 0, index))
    ml_spec = pl.BlockSpec((heads, 1, tq), lambda qi, b, info: (index, 0, qi))
    acc_spec = pl.BlockSpec((width, tq), lambda qi, b, info: (index, qi))
    in_specs = [q_spec, k_spec, v_spec]
    args = [queries, keys, values]
    if not first:
        in_specs += [ml_spec, ml_spec, acc_spec]
        args += list(state)
    if last:
        out_shape = jax.ShapeDtypeStruct((width, tok), jnp.bfloat16)
        out_specs = pl.BlockSpec((width, tq), lambda qi, b, info: (0, qi))
    else:
        out_shape = (
            jax.ShapeDtypeStruct((heads * nparts, 1, tok), jnp.float32),
            jax.ShapeDtypeStruct((heads * nparts, 1, tok), jnp.float32),
            jax.ShapeDtypeStruct((width * nparts, tok), jnp.float32),
        )
        out_specs = (ml_spec, ml_spec, acc_spec)
    flops = 32 * 4 * tok * nb * tk * width * 2
    cost = pl.CostEstimate(
        flops=flops,
        transcendentals=tok * nb * tk * heads,
        bytes_accessed=2 * (tok * width * 2 + 2 * nb * tk * width * 2 + tok * width * 4),
    )
    return pl.pallas_call(
        kernel,
        out_shape=out_shape,
        grid_spec=pltpu.PrefetchScalarGridSpec(
            num_scalar_prefetch=1,
            grid=(tok // tq, nb),
            in_specs=in_specs,
            out_specs=out_specs,
            scratch_shapes=[
                pltpu.VMEM((heads, 1, tq), jnp.float32),
                pltpu.VMEM((heads, 1, tq), jnp.float32),
                pltpu.VMEM((width, tq), jnp.float32),
            ],
        ),
        compiler_params=pltpu.CompilerParams(dimension_semantics=("arbitrary", "arbitrary")),
        cost_estimate=cost,
    )(info, *args)


def local(q_img, k_img, v_img, text_keys, text_values, text_lengths, img_lengths, out_weight):
    tok_dev = q_img.shape[1]
    width = q_img.shape[2]
    reqs = text_keys.shape[1]
    text_slots = text_keys.shape[2]
    nseq = lax.axis_size("seq")
    me = lax.axis_index("seq")
    total = tok_dev * nseq
    longest = total // 2
    reach = min(nseq - 1, (longest + tok_dev - 2) // tok_dev)
    ends = jnp.cumsum(img_lengths).astype(jnp.int32)
    queries = q_img[0]

    def info_for(kstart):
        head = jnp.stack([me * tok_dev, kstart]).astype(jnp.int32)
        return jnp.concatenate([head, ends, text_lengths[0].astype(jnp.int32)])

    pad_to = -(-text_slots // 128) * 128
    pad = ((0, 0), (0, pad_to - text_slots), (0, 0))
    tk = min(tok_dev, 128)
    sub = pad_to // tk
    text_k = jnp.pad(text_keys[0], pad).reshape(reqs * sub, tk, width)
    text_v = jnp.pad(text_values[0], pad).reshape(reqs * sub, tk, width)

    def as_blocks(x):
        return x.reshape(2 * tok_dev // tk, tk, width)

    common = dict(reqs=reqs, total=total)
    state = attend_chunk(info_for(0), queries, text_k, text_v, 0, None, kind="text", last=False, sub=sub, **common)
    both = jnp.stack([k_img[0], v_img[0]])
    chunks = [(both, me * tok_dev)]
    to_right = [(i, i + 1) for i in range(nseq - 1)]
    to_left = [(i + 1, i) for i in range(nseq - 1)]
    from_left, from_right = both, both
    for step in range(1, reach + 1):
        from_left = lax.ppermute(from_left, "seq", to_right)
        from_right = lax.ppermute(from_right, "seq", to_left)
        chunks.append((from_left, (me - step) * tok_dev))
        chunks.append((from_right, (me + step) * tok_dev))
    for index, (kv, lower) in enumerate(chunks[:-1]):
        blocks = as_blocks(kv)
        state = attend_chunk(
            info_for(lower), queries, blocks, blocks, tok_dev // tk, state, kind="image", last=False,
            **common,
        )
    kv, lower = chunks[-1]
    nhead = lax.axis_size("head")
    nparts = 2 if nhead == 2 and width % 256 == 0 else 1
    attn_parts = [
        attend_chunk(
            info_for(lower), queries, as_blocks(kv), as_blocks(kv), tok_dev // tk, state, kind="image", last=True,
            part=(i, nparts), **common,
        )
        for i in range(nparts)
    ]
    own_cfg = lax.axis_index("cfg")
    cols = out_weight.shape[1]
    half = cols // 2
    mine_weight = jnp.where(own_cfg == 0, guidance, 1.0 - guidance)
    w_keep = lax.dynamic_slice_in_dim(out_weight, own_cfg * half, half, 1)
    w_out = lax.dynamic_slice_in_dim(out_weight, (1 - own_cfg) * half, half, 1)
    if nhead == 2:
        hx = lax.axis_index("head")
        others = [partner_2(x, "head", 0) for x in attn_parts]
        piece = width // nparts

        def project(w):
            own = None
            for i, x in enumerate(attn_parts):
                term = lax.dot_general(
                    x, lax.dynamic_slice_in_dim(w, hx * width + i * piece, piece, 0),
                    (((0,), (0,)), ((), ())), preferred_element_type=jnp.float32,
                )
                own = term if own is None else own + term
            summed = lax.optimization_barrier(own)
            for i, x in enumerate(others):
                summed = summed + lax.dot_general(
                    x, lax.dynamic_slice_in_dim(w, (1 - hx) * width + i * piece, piece, 0),
                    (((0,), (0,)), ((), ())), preferred_element_type=jnp.float32,
                )
            return summed
    else:
        gathered = lax.all_gather(jnp.concatenate(attn_parts, axis=0), "head", axis=0, tiled=True)

        def project(w):
            return lax.dot_general(gathered, w, (((0,), (0,)), ((), ())), preferred_element_type=jnp.float32)

    outgoing = project(w_out)
    partner = partner_2(outgoing.astype(jnp.bfloat16), "cfg", 0).astype(outgoing.dtype)
    keep = project(w_keep)
    guided = mine_weight * keep + (1.0 - mine_weight) * partner
    return guided.astype(jnp.bfloat16)


def solution(mesh):
    placed = (
        P("cfg", ("groups", "seq"), "head"),
        P("cfg", ("groups", "seq"), "head"),
        P("cfg", ("groups", "seq"), "head"),
        P("cfg", "groups", None, "head"),
        P("cfg", "groups", None, "head"),
        P("cfg", "groups"),
        P("groups"),
        P(None, "head"),
    )
    return jax.shard_map(
        local,
        mesh=mesh,
        in_specs=placed,
        out_specs=P(("groups", "seq"), ("head", "cfg")),
        check_vma=False,
    )
```

profile of v0, /device:TPU:11, one launch (start us, length us, event | category | flops | bytes accessed | tf_op | source)
XLA Modules:
  0.0 156.3 jit_solution(13564209403973421167)
XLA Ops:
  0.0 0.0 copy-start.5
  0.0 0.0 copy-start.1
  0.0 2.2 %constant_dynamic-update-slice_fusion.1 = bf16[2,512,768]{2,1,0:T(8,128)(2,1)} fusion(bf16[1,512,768]{2,1,0:T(8,128)(2,1)} %param.9), kind=kLoop, calls=%fused_computation.19 | loop fusion | bytes 1572864
  2.2 0.0 copy-done.5
  2.2 0.9 constant_dynamic-update-slice_fusion
  3.2 3.2 %collective-permute-start.2 = (bf16[2,512,768]{2,1,0:T(8,128)(2,1)}, bf16[2,512,768]{2,1,0:T(8,128)(2,1)}, u32[]{:S(2)}, u32[]{:S(2)}) collective-permute-start(bf16[2,512,768]{2,1,0:T(8,128)(2,1)} %constant_dynamic-update-slice_fusion), channel_id=1, source_target_pairs={{0,4},{4,8},{8,12},{1,5},{5,9},{9,13},{2,6},{6,10},{10,14},{3,7},{... | collective-permute-start | bytes 4718600 | tf_op jit(solution)/shard_map/ppermute | solution.py:219
  6.4 3.2 %collective-permute-start = (bf16[2,512,768]{2,1,0:T(8,128)(2,1)}, bf16[2,512,768]{2,1,0:T(8,128)(2,1)}, u32[]{:S(2)}, u32[]{:S(2)}) collective-permute-start(bf16[2,512,768]{2,1,0:T(8,128)(2,1)} %constant_dynamic-update-slice_fusion), channel_id=1, source_target_pairs={{4,0},{8,4},{12,8},{5,1},{9,5},{13,9},{6,2},{10,6},{14,10},{7,3},{... | collective-permute-start | bytes 4718600 | tf_op jit(solution)/shard_map/ppermute | solution.py:220
  9.6 0.0 copy-done.1
  9.6 0.0 copy-start.2
  9.6 0.3 copy.11
  9.9 1.3 copy-done.2
  11.2 0.3 copy.12
  11.4 1.6 %pad.7.clone = bf16[4,384,768]{2,1,0:T(8,128)(2,1)} pad(bf16[4,333,768]{2,1,0:T(8,128)(2,1)S(1)} %copy.11, bf16[]{:T(256)} %constant.121.clone.1), padding=0_0x0_51x0_0 | pad | bytes 4405250 | tf_op jit(solution)/shard_map/jit(_pad)/pad | solution.py:205
  13.0 0.0 copy-start.12
  13.0 1.6 %pad.8.clone = bf16[4,384,768]{2,1,0:T(8,128)(2,1)} pad(bf16[4,333,768]{2,1,0:T(8,128)(2,1)S(1)} %copy.12, bf16[]{:T(256)} %constant.121.clone.1), padding=0_0x0_51x0_0 | pad | bytes 4405250 | tf_op jit(solution)/shard_map/jit(_pad)/pad | solution.py:206
  14.6 0.0 copy-done.12
  14.6 0.2 reduce-window.9
  14.8 0.0 copy-done.6
  14.8 0.7 add_add_fusion.4
  15.5 0.7 add_add_fusion.5
  16.1 20.8 %shard_map.82 = (f32[12,1,512]{2,1,0:T(1,128)}, f32[12,1,512]{2,1,0:T(1,128)}, f32[768,512]{1,0:T(8,128)}) custom-call(s32[10]{0:T(128)} %get-tuple-element.35.info_ref, bf16[512,768]{1,0:T(8,128)(2,1)} %bitcast.42, bf16[12,128,768]{2,1,0:T(8,128)(2,1)} %bitcast.26, bf16[12,128,768]{2,1,0:T(8,128)(2,1)} %bitcast.27), custom_call_target="tpu_custom_call" | custom-call | flops 154618822656 | bytes 14155776 | tf_op jit(solution)/shard_map/pallas_call | solution.py:165
  36.9 0.0 copy-done.8
  36.9 0.0 copy-start.7
  36.9 0.0 copy-start.9
  36.9 12.9 %shard_map.83 = (f32[12,1,512]{2,1,0:T(1,128)}, f32[12,1,512]{2,1,0:T(1,128)}, f32[768,512]{1,0:T(8,128)}) custom-call(s32[10]{0:T(128)} %get-tuple-element.37.info_ref, bf16[512,768]{1,0:T(8,128)(2,1)} %bitcast.43, bf16[8,128,768]{2,1,0:T(8,128)(2,1)} %bitcast.13.k_ref.v_ref, bf16[8,128,768]{2,1,0:T(8,128)(2,1)} %bitcast.13.k_ref.v_ref, ...), custom_call_target="tpu_custom_call" | custom-call | flops 51539607552 | bytes 7864320 | tf_op jit(solution)/shard_map/pallas_call | solution.py:165
  49.9 0.0 copy-done.7
  49.9 0.0 copy-done.9
  49.9 0.7 add_add_fusion.3
  50.6 0.0 collective-permute-done.2
  50.6 10.8 %shard_map.84 = (f32[12,1,512]{2,1,0:T(1,128)}, f32[12,1,512]{2,1,0:T(1,128)}, f32[768,512]{1,0:T(8,128)}) custom-call(s32[10]{0:T(128)} %get-tuple-element.39.info_ref, bf16[512,768]{1,0:T(8,128)(2,1)} %bitcast.44, bf16[8,128,768]{2,1,0:T(8,128)(2,1)} %bitcast.12.k_ref.v_ref, bf16[8,128,768]{2,1,0:T(8,128)(2,1)} %bitcast.12.k_ref.v_ref, ...), custom_call_target="tpu_custom_call" | custom-call | flops 51539607552 | bytes 7864320 | tf_op jit(solution)/shard_map/pallas_call | solution.py:165
  61.3 1.9 %collective-permute-start.3 = (bf16[2,512,768]{2,1,0:T(8,128)(2,1)}, bf16[2,512,768]{2,1,0:T(8,128)(2,1)S(1)}, u32[]{:S(2)}, u32[]{:S(2)}) collective-permute-start(bf16[2,512,768]{2,1,0:T(8,128)(2,1)} %collective-permute-done.2), channel_id=1, source_target_pairs={{0,4},{4,8},{8,12},{1,5},{5,9},{9,13},{2,6},{6,10},{10,14},{3,7},{... | collective-permute-start | bytes 4718600 | tf_op jit(solution)/shard_map/ppermute | solution.py:219
  63.2 0.0 collective-permute-done
  63.2 10.7 %shard_map.85 = (f32[12,1,512]{2,1,0:T(1,128)}, f32[12,1,512]{2,1,0:T(1,128)}, f32[768,512]{1,0:T(8,128)}) custom-call(s32[10]{0:T(128)} %get-tuple-element.38.info_ref, bf16[512,768]{1,0:T(8,128)(2,1)} %bitcast.45, bf16[8,128,768]{2,1,0:T(8,128)(2,1)} %bitcast.10.k_ref.v_ref, bf16[8,128,768]{2,1,0:T(8,128)(2,1)} %bitcast.10.k_ref.v_ref, ...), custom_call_target="tpu_custom_call" | custom-call | flops 51539607552 | bytes 7864320 | tf_op jit(solution)/shard_map/pallas_call | solution.py:165
  73.9 2.6 %collective-permute-start.1 = (bf16[2,512,768]{2,1,0:T(8,128)(2,1)}, bf16[2,512,768]{2,1,0:T(8,128)(2,1)S(1)}, u32[]{:S(2)}, u32[]{:S(2)}) collective-permute-start(bf16[2,512,768]{2,1,0:T(8,128)(2,1)} %collective-permute-done), channel_id=1, source_target_pairs={{4,0},{8,4},{12,8},{5,1},{9,5},{13,9},{6,2},{10,6},{14,10},{7,3},{... | collective-permute-start | bytes 4718600 | tf_op jit(solution)/shard_map/ppermute | solution.py:220
  76.5 22.6 %collective-permute-done.3 = bf16[2,512,768]{2,1,0:T(8,128)(2,1)S(1)} collective-permute-done((bf16[2,512,768]{2,1,0:T(8,128)(2,1)}, bf16[2,512,768]{2,1,0:T(8,128)(2,1)S(1)}, u32[]{:S(2)}, u32[]{:S(2)}) %collective-permute-start.3) | collective-permute-done | bytes 1572896 | tf_op jit(solution)/shard_map/ppermute | solution.py:219
  99.1 0.0 copy-start.10
  99.1 1.2 copy-done.10
  100.2 7.5 %shard_map.86 = (f32[12,1,512]{2,1,0:T(1,128)}, f32[12,1,512]{2,1,0:T(1,128)}, f32[768,512]{1,0:T(8,128)}) custom-call(s32[10]{0:T(128)} %get-tuple-element.36.info_ref, bf16[512,768]{1,0:T(8,128)(2,1)} %bitcast.46, bf16[8,128,768]{2,1,0:T(8,128)(2,1)} %bitcast.36, bf16[8,128,768]{2,1,0:T(8,128)(2,1)} %bitcast.37, f32[12,1,512]{2,1,0:T(1,128)} %get-tuple-element.29.refs_0_, ...), custom_call_target="tpu_custom_call" | custom-call | flops 51539607552 | bytes 7864320 | tf_op jit(solution)/shard_map/pallas_call | solution.py:165
  107.7 7.9 %collective-permute-done.1 = bf16[2,512,768]{2,1,0:T(8,128)(2,1)S(1)} collective-permute-done((bf16[2,512,768]{2,1,0:T(8,128)(2,1)}, bf16[2,512,768]{2,1,0:T(8,128)(2,1)S(1)}, u32[]{:S(2)}, u32[]{:S(2)}) %collective-permute-start.1) | collective-permute-done | bytes 1572896 | tf_op jit(solution)/shard_map/ppermute | solution.py:220
  115.6 0.0 copy-start.11
  115.6 1.2 copy-done.11
  116.8 7.6 %shard_map.87 = bf16[384,512]{1,0:T(8,128)(2,1)} custom-call(s32[10]{0:T(128)} %get-tuple-element.40.info_ref, bf16[512,768]{1,0:T(8,128)(2,1)} %bitcast.47, bf16[8,128,768]{2,1,0:T(8,128)(2,1)} %bitcast.38, bf16[8,128,768]{2,1,0:T(8,128)(2,1)} %bitcast.39, f32[12,1,512]{2,1,0:T(1,128)} %get-tuple-element.32.refs_0_, ...), custom_call_target="tpu_custom_call" | custom-call | flops 25769803776 | bytes 3932160 | tf_op jit(solution)/shard_map/pallas_call | solution.py:165
  124.4 0.0 copy-start.3
  124.4 7.7 %shard_map.88 = bf16[384,512]{1,0:T(8,128)(2,1)} custom-call(s32[10]{0:T(128)} %get-tuple-element.40.info_ref, bf16[512,768]{1,0:T(8,128)(2,1)} %bitcast.48, bf16[8,128,768]{2,1,0:T(8,128)(2,1)} %bitcast.40, bf16[8,128,768]{2,1,0:T(8,128)(2,1)} %bitcast.41, f32[12,1,512]{2,1,0:T(1,128)} %get-tuple-element.32.refs_0_, ...), custom_call_target="tpu_custom_call" | custom-call | flops 25769803776 | bytes 3932160 | tf_op jit(solution)/shard_map/pallas_call | solution.py:165
  132.1 0.0 copy-done.3
  132.1 0.3 collective-permute-start.4
  132.4 1.2 collective-permute-start.5
  133.6 1.8 %fusion.4 = f32[512,608]{0,1:T(8,128)S(1)} fusion(bf16[384,512]{1,0:T(8,128)(2,1)} %shard_map.88, bf16[1536,1216]{0,1:T(8,128)(2,1)} %param.15, s32[]{:T(128)S(6)} %select_n.44, s32[]{:T(128)S(6)} %select_n.50), kind=kOutput, calls=%fused_computation.8 | convolution fusion | flops 239075328 | bytes 2105352 | tf_op jit(solution)/shard_map/dot_general | solution.py:253
  135.4 0.0 copy-start.4
  135.5 1.7 %convolution_add_fusion = f32[512,608]{0,1:T(8,128)S(1)} fusion(f32[512,608]{0,1:T(8,128)S(1)} %fusion.4, bf16[384,512]{1,0:T(8,128)(2,1)S(1)} %copy-done.3, bf16[1536,1216]{0,1:T(8,128)(2,1)} %param.15, s32[]{:T(128)S(6)} %select_n.40, s32[]{:T(128)S(6)} %select_n.50), kind=kOutput, calls=%fused_computation | convolution fusion | flops 239386624 | bytes 3350536 | tf_op jit(solution)/shard_map/dot_general | solution.py:253
  137.1 0.0 copy-done
  137.1 0.0 copy-done.4
  137.2 0.6 fusion.11
  137.7 4.7 %collective-permute-done.4 = bf16[384,512]{1,0:T(8,128)(2,1)S(1)} collective-permute-done((bf16[384,512]{1,0:T(8,128)(2,1)S(1)}, bf16[384,512]{1,0:T(8,128)(2,1)S(1)}, u32[]{:S(2)}, u32[]{:S(2)}) %collective-permute-start.4) | collective-permute-done | bytes 393248 | tf_op jit(solution)/shard_map/ppermute | solution.py:19
  142.4 0.5 fusion.2
  143.0 7.9 %collective-permute-done.5 = bf16[384,512]{1,0:T(8,128)(2,1)S(1)} collective-permute-done((bf16[384,512]{1,0:T(8,128)(2,1)}, bf16[384,512]{1,0:T(8,128)(2,1)S(1)}, u32[]{:S(2)}, u32[]{:S(2)}) %collective-permute-start.5) | collective-permute-done | bytes 393248 | tf_op jit(solution)/shard_map/ppermute | solution.py:19
  150.8 0.6 fusion
  151.4 0.5 add_convert_fusion.1
  151.9 1.3 collective-permute-start.6
  153.2 0.6 convolution_add_fusion.1
  153.8 0.5 fusion.9
  154.3 0.6 fusion.7
  154.9 0.0 collective-permute-done.6
  154.9 1.4 add_convert_fusion
  (3 shorter events, 0.0 us)
Async XLA Ops:
  0.0 2.2 %copy-start.5 = (bf16[1,512,768]{2,1,0:T(8,128)(2,1)S(1)}, bf16[1,512,768]{2,1,0:T(8,128)(2,1)}, u32[]{:S(2)}) copy-start(bf16[1,512,768]{2,1,0:T(8,128)(2,1)} %param.10) | copy-start | bytes 2359300
  0.0 9.6 %copy-start.1 = (bf16[1,4,333,768]{3,1,2,0:T(4,128)(2,1)S(1)}, bf16[1,4,333,768]{3,1,2,0:T(4,128)(2,1)}, u32[]{:S(2)}) copy-start(bf16[1,4,333,768]{3,1,2,0:T(4,128)(2,1)} %param.11) | copy-start | bytes 6137860
  3.2 47.4 %collective-permute-start.2 = (bf16[2,512,768]{2,1,0:T(8,128)(2,1)}, bf16[2,512,768]{2,1,0:T(8,128)(2,1)}, u32[]{:S(2)}, u32[]{:S(2)}) collective-permute-start(bf16[2,512,768]{2,1,0:T(8,128)(2,1)} %constant_dynamic-update-slice_fusion), channel_id=1, source_target_pairs={{0,4},{4,8},{8,12},{1,5},{5,9},{9,13},{2,6},{6,10},{10,14},{3,7},{... | collective-permute-start | bytes 4718600 | tf_op jit(solution)/shard_map/ppermute | solution.py:219
  6.4 56.9 %collective-permute-start = (bf16[2,512,768]{2,1,0:T(8,128)(2,1)}, bf16[2,512,768]{2,1,0:T(8,128)(2,1)}, u32[]{:S(2)}, u32[]{:S(2)}) collective-permute-start(bf16[2,512,768]{2,1,0:T(8,128)(2,1)} %constant_dynamic-update-slice_fusion), channel_id=1, source_target_pairs={{4,0},{8,4},{12,8},{5,1},{9,5},{13,9},{6,2},{10,6},{14,10},{7,3},{... | collective-permute-start | bytes 4718600 | tf_op jit(solution)/shard_map/ppermute | solution.py:220
  9.6 1.6 %copy-start.2 = (bf16[1,4,333,768]{3,1,2,0:T(4,128)(2,1)S(1)}, bf16[1,4,333,768]{3,1,2,0:T(4,128)(2,1)}, u32[]{:S(2)}) copy-start(bf16[1,4,333,768]{3,1,2,0:T(4,128)(2,1)} %param.12) | copy-start | bytes 6137860
  13.0 1.6 %copy-start.12 = (s32[4]{0:T(128)S(1)}, s32[4]{0:T(128)}, u32[]{:S(2)}) copy-start(s32[4]{0:T(128)} %param.14) | copy-start | bytes 52
  13.0 1.8 %copy-start.6 = (s32[1,4]{1,0:T(1,128)S(1)}, s32[1,4]{1,0:T(1,128)}, u32[]{:S(2)}) copy-start(s32[1,4]{1,0:T(1,128)} %param.13) | copy-start | bytes 52
  14.8 22.1 %copy-start.8 = (s32[4,1]{0,1:T(1,128)}, s32[4,1]{0,1:T(1,128)S(1)}, u32[]{:S(2)}) copy-start(s32[4,1]{0,1:T(1,128)S(1)} %reduce-window.9) | copy-start | bytes 52
  36.9 13.0 %copy-start.7 = (s32[1,4]{1,0:T(1,128)S(1)}, s32[1,4]{1,0:T(1,128)}, u32[]{:S(2)}) copy-start(s32[1,4]{1,0:T(1,128)} %param.13) | copy-start | bytes 52
  36.9 13.0 %copy-start.9 = (s32[4,1]{0,1:T(1,128)S(1)}, s32[4,1]{0,1:T(1,128)}, u32[]{:S(2)}) copy-start(s32[4,1]{0,1:T(1,128)} %copy-done.8) | copy-start | bytes 52
  61.3 37.7 %collective-permute-start.3 = (bf16[2,512,768]{2,1,0:T(8,128)(2,1)}, bf16[2,512,768]{2,1,0:T(8,128)(2,1)S(1)}, u32[]{:S(2)}, u32[]{:S(2)}) collective-permute-start(bf16[2,512,768]{2,1,0:T(8,128)(2,1)} %collective-permute-done.2), channel_id=1, source_target_pairs={{0,4},{4,8},{8,12},{1,5},{5,9},{9,13},{2,6},{6,10},{10,14},{3,7},{... | collective-permute-start | bytes 4718600 | tf_op jit(solution)/shard_map/ppermute | solution.py:219
  73.9 41.7 %collective-permute-start.1 = (bf16[2,512,768]{2,1,0:T(8,128)(2,1)}, bf16[2,512,768]{2,1,0:T(8,128)(2,1)S(1)}, u32[]{:S(2)}, u32[]{:S(2)}) collective-permute-start(bf16[2,512,768]{2,1,0:T(8,128)(2,1)} %collective-permute-done), channel_id=1, source_target_pairs={{4,0},{8,4},{12,8},{5,1},{9,5},{13,9},{6,2},{10,6},{14,10},{7,3},{... | collective-permute-start | bytes 4718600 | tf_op jit(solution)/shard_map/ppermute | solution.py:220
  99.1 1.2 copy-start.10
  115.6 1.2 copy-start.11
  124.4 7.8 %copy-start.3 = (bf16[384,512]{1,0:T(8,128)(2,1)S(1)}, bf16[384,512]{1,0:T(8,128)(2,1)}, u32[]{:S(2)}) copy-start(bf16[384,512]{1,0:T(8,128)(2,1)} %shard_map.87) | copy-start | bytes 1179652
  132.1 10.3 %collective-permute-start.4 = (bf16[384,512]{1,0:T(8,128)(2,1)S(1)}, bf16[384,512]{1,0:T(8,128)(2,1)S(1)}, u32[]{:S(2)}, u32[]{:S(2)}) collective-permute-start(bf16[384,512]{1,0:T(8,128)(2,1)S(1)} %copy-done.3), channel_id=1, source_target_pairs={{0,2},{2,0},{1,3},{3,1},{4,6},{6,4},{5,7},{7,5},{8,10},{10,8},{9,1... | collective-permute-start | bytes 1179656 | tf_op jit(solution)/shard_map/ppermute | solution.py:19
  132.4 18.5 %collective-permute-start.5 = (bf16[384,512]{1,0:T(8,128)(2,1)}, bf16[384,512]{1,0:T(8,128)(2,1)S(1)}, u32[]{:S(2)}, u32[]{:S(2)}) collective-permute-start(bf16[384,512]{1,0:T(8,128)(2,1)} %shard_map.88), channel_id=1, source_target_pairs={{0,2},{2,0},{1,3},{3,1},{4,6},{6,4},{5,7},{7,5},{8,10},{10,8},{9,1... | collective-permute-start | bytes 1179656 | tf_op jit(solution)/shard_map/ppermute | solution.py:19
  133.6 3.5 %copy-start = (bf16[1536,1216]{0,1:T(8,128)(2,1)S(1)}, bf16[1536,1216]{0,1:T(8,128)(2,1)}, u32[]{:S(2)}) copy-start(bf16[1536,1216]{0,1:T(8,128)(2,1)} %param.15) | copy-start | bytes 11206660
  135.4 1.7 %copy-start.4 = (bf16[384,512]{1,0:T(8,128)(2,1)S(1)}, bf16[384,512]{1,0:T(8,128)(2,1)}, u32[]{:S(2)}) copy-start(bf16[384,512]{1,0:T(8,128)(2,1)} %shard_map.88) | copy-start | bytes 1179652
  151.9 3.0 %collective-permute-start.6 = (bf16[512,608]{0,1:T(8,128)(2,1)S(1)}, bf16[512,608]{0,1:T(8,128)(2,1)S(1)}, u32[]{:S(2)}, u32[]{:S(2)}) collective-permute-start(bf16[512,608]{0,1:T(8,128)(2,1)S(1)} %add_convert_fusion.1), channel_id=1, source_target_pairs={{0,1},{1,0},{2,3},{3,2},{4,5},{5,4},{6,7},{7,6},{8,9},{9,8},{10,11... | collective-permute-start | bytes 1867784 | tf_op jit(solution)/shard_map/ppermute | solution.py:19
where the time goes:
time: 155 us; the launch traced here: 156 us
  Pallas kernels  78 us (50%)
  waiting for transfers between devices  43.1 us (28%)
  starting transfers between devices  13.7 us (9%)
  local copies, waits for them, and re-layouts  10.5 us (7%)
  matrix products  6.82 us (4%)
  other arithmetic  3.99 us (3%)
    pallas_call x7, Pallas kernels, attend_chunk(): pl.pallas_call(kernel, out_shape=out_shape, grid_spec=pltpu.PrefetchScala...  78 us
    ppermute x2, waiting for transfers between devices, local(): from_left = lax.ppermute(from_left, 'seq', to_right)  22.6 us
    ppermute x3, waiting for transfers between devices, partner_2(): lax.ppermute(x, axis, [(i, i ^ 1 << distance) for i in range(lax.axis_siz...  12.6 us
    ppermute x2, waiting for transfers between devices, local(): from_right = lax.ppermute(from_right, 'seq', to_left)  7.9 us
    unnamed x29, local copies, waits for them, and re-layouts  6.41 us
    ppermute x2, starting transfers between devices, local(): from_right = lax.ppermute(from_right, 'seq', to_left)  5.81 us
    ppermute x2, starting transfers between devices, local(): from_left = lax.ppermute(from_left, 'seq', to_right)  5.1 us
    dot_general x4, matrix products, project(): lax.dot_general(x, lax.dynamic_slice_in_dim(w, hx * width + i * piece, pi...  4.62 us
  transfers between devices with their start and end apart: 7, of which 4 were waited for; matrix products, arithmetic and copies ran while one was open for 8% of the time, Pallas kernels for 40%

commit v1 on v0

--- a/solution.py
+++ b/solution.py
@@ -218,6 +218,9 @@
     for step in range(1, reach + 1):
         from_left = lax.ppermute(from_left, "seq", to_right)
         from_right = lax.ppermute(from_right, "seq", to_left)
+        if step == 1:
+            local_kv, from_left, from_right = lax.optimization_barrier((both, from_left, from_right))
+            chunks[0] = (local_kv, me * tok_dev)
         chunks.append((from_left, (me - step) * tok_dev))
         chunks.append((from_right, (me + step) * tok_dev))
     for index, (kv, lower) in enumerate(chunks[:-1]):

time: 155 us -> 133 us (0.86)
  the two profiles are of different devices: /device:TPU:11 before, /device:TPU:15 now
where the time goes in v1:
time: 133 us
  Pallas kernels  77.7 us (58%)
  starting transfers between devices  17.9 us (13%)
  waiting for transfers between devices  17.2 us (13%)
  local copies, waits for them, and re-layouts  8.2 us (6%)
  matrix products  6.83 us (5%)
  other arithmetic  4.8 us (4%)
    pallas_call x7, Pallas kernels, attend_chunk(): pl.pallas_call(kernel, out_shape=out_shape, grid_spec=pltpu.PrefetchScala...  77.7 us
    ppermute x3, waiting for transfers between devices, partner_2(): lax.ppermute(x, axis, [(i, i ^ 1 << distance) for i in range(lax.axis_siz...  10.5 us
    ppermute x2, starting transfers between devices, local(): from_right = lax.ppermute(from_right, 'seq', to_left)  6.61 us
    ppermute x2, starting transfers between devices, local(): from_left = lax.ppermute(from_left, 'seq', to_right)  6.39 us
    ppermute x3, starting transfers between devices, partner_2(): lax.ppermute(x, axis, [(i, i ^ 1 << distance) for i in range(lax.axis_siz...  4.87 us
    dot_general x4, matrix products, project(): lax.dot_general(x, lax.dynamic_slice_in_dim(w, hx * width + i * piece, pi...  4.61 us
    unnamed x23, local copies, waits for them, and re-layouts  4.07 us
    ppermute x2, waiting for transfers between devices, local(): from_left = lax.ppermute(from_left, 'seq', to_right)  3.81 us
  transfers between devices with their start and end apart: 7, of which 4 were waited for; matrix products, arithmetic and copies ran while one was open for 10% of the time, Pallas kernels for 46%

profile of v1, /device:TPU:15, one launch (start us, length us, event | category | flops | bytes accessed | tf_op | source)
XLA Modules:
  0.0 132.8 jit_solution(14245802927019051977)
XLA Ops:
  0.0 0.0 copy-start.5
  0.0 0.0 copy-start.1
  0.0 2.2 %constant_dynamic-update-slice_fusion.1 = bf16[2,512,768]{2,1,0:T(8,128)(2,1)} fusion(bf16[1,512,768]{2,1,0:T(8,128)(2,1)} %param.9), kind=kLoop, calls=%fused_computation.19 | loop fusion | bytes 1572864
  2.2 0.0 copy-done.5
  2.2 0.9 constant_dynamic-update-slice_fusion
  3.2 3.2 %collective-permute-start = (bf16[2,512,768]{2,1,0:T(8,128)(2,1)}, bf16[2,512,768]{2,1,0:T(8,128)(2,1)}, u32[]{:S(2)}, u32[]{:S(2)}) collective-permute-start(bf16[2,512,768]{2,1,0:T(8,128)(2,1)} %constant_dynamic-update-slice_fusion), channel_id=1, source_target_pairs={{0,4},{4,8},{8,12},{1,5},{5,9},{9,13},{2,6},{6,10},{10,14},{3,7},{... | collective-permute-start | bytes 4718600 | tf_op jit(solution)/shard_map/ppermute | solution.py:219
  6.4 3.2 %collective-permute-start.1 = (bf16[2,512,768]{2,1,0:T(8,128)(2,1)}, bf16[2,512,768]{2,1,0:T(8,128)(2,1)}, u32[]{:S(2)}, u32[]{:S(2)}) collective-permute-start(bf16[2,512,768]{2,1,0:T(8,128)(2,1)} %constant_dynamic-update-slice_fusion), channel_id=1, source_target_pairs={{4,0},{8,4},{12,8},{5,1},{9,5},{13,9},{6,2},{10,6},{14,10},{7,3},{... | collective-permute-start | bytes 4718600 | tf_op jit(solution)/shard_map/ppermute | solution.py:220
  9.6 0.0 copy-done.1
  9.6 0.0 copy-start.2
  9.6 0.3 copy.11
  9.9 1.3 copy-done.2
  11.2 0.3 copy.12
  11.4 1.6 %pad.7.clone = bf16[4,384,768]{2,1,0:T(8,128)(2,1)} pad(bf16[4,333,768]{2,1,0:T(8,128)(2,1)S(1)} %copy.11, bf16[]{:T(256)} %constant.121.clone.1), padding=0_0x0_51x0_0 | pad | bytes 4405250 | tf_op jit(solution)/shard_map/jit(_pad)/pad | solution.py:205
  13.1 0.0 copy-start.9
  13.1 0.0 copy-start.6
  13.1 1.6 %pad.8.clone = bf16[4,384,768]{2,1,0:T(8,128)(2,1)} pad(bf16[4,333,768]{2,1,0:T(8,128)(2,1)S(1)} %copy.12, bf16[]{:T(256)} %constant.121.clone.1), padding=0_0x0_51x0_0 | pad | bytes 4405250 | tf_op jit(solution)/shard_map/jit(_pad)/pad | solution.py:206
  14.7 0.0 copy-done.9
  14.7 0.2 reduce-window.9
  14.8 0.0 copy-start.8
  14.8 0.0 copy-done.6
  14.8 0.7 add_add_fusion.5
  15.5 0.0 copy-start.7
  15.5 18.7 %shard_map.82 = (f32[12,1,512]{2,1,0:T(1,128)}, f32[12,1,512]{2,1,0:T(1,128)}, f32[768,512]{1,0:T(8,128)}) custom-call(s32[10]{0:T(128)} %get-tuple-element.41.info_ref, bf16[512,768]{1,0:T(8,128)(2,1)} %bitcast.36, bf16[12,128,768]{2,1,0:T(8,128)(2,1)} %bitcast.26, bf16[12,128,768]{2,1,0:T(8,128)(2,1)} %bitcast.27), custom_call_target="tpu_custom_call" | custom-call | flops 154618822656 | bytes 14155776 | tf_op jit(solution)/shard_map/pallas_call | solution.py:165
  34.2 0.0 copy-done.8
  34.2 0.0 copy-done.7
  34.2 1.3 add_add_fusion.4
  35.5 1.3 add_add_fusion.3
  36.8 3.8 %collective-permute-done = bf16[2,512,768]{2,1,0:T(8,128)(2,1)} collective-permute-done((bf16[2,512,768]{2,1,0:T(8,128)(2,1)}, bf16[2,512,768]{2,1,0:T(8,128)(2,1)}, u32[]{:S(2)}, u32[]{:S(2)}) %collective-permute-start) | collective-permute-done | bytes 1572896 | tf_op jit(solution)/shard_map/ppermute | solution.py:219
  40.6 2.9 %collective-permute-done.1 = bf16[2,512,768]{2,1,0:T(8,128)(2,1)} collective-permute-done((bf16[2,512,768]{2,1,0:T(8,128)(2,1)}, bf16[2,512,768]{2,1,0:T(8,128)(2,1)}, u32[]{:S(2)}, u32[]{:S(2)}) %collective-permute-start.1) | collective-permute-done | bytes 1572896 | tf_op jit(solution)/shard_map/ppermute | solution.py:220
  43.5 3.2 %collective-permute-start.3 = (bf16[2,512,768]{2,1,0:T(8,128)(2,1)}, bf16[2,512,768]{2,1,0:T(8,128)(2,1)}, u32[]{:S(2)}, u32[]{:S(2)}) collective-permute-start(bf16[2,512,768]{2,1,0:T(8,128)(2,1)} %collective-permute-done), channel_id=1, source_target_pairs={{0,4},{4,8},{8,12},{1,5},{5,9},{9,13},{2,6},{6,10},{10,14},{3,7},{... | collective-permute-start | bytes 4718600 | tf_op jit(solution)/shard_map/ppermute | solution.py:219
  46.7 3.4 %collective-permute-start.2 = (bf16[2,512,768]{2,1,0:T(8,128)(2,1)}, bf16[2,512,768]{2,1,0:T(8,128)(2,1)}, u32[]{:S(2)}, u32[]{:S(2)}) collective-permute-start(bf16[2,512,768]{2,1,0:T(8,128)(2,1)} %collective-permute-done.1), channel_id=1, source_target_pairs={{4,0},{8,4},{12,8},{5,1},{9,5},{13,9},{6,2},{10,6},{14,10},{7,3},{... | collective-permute-start | bytes 4718600 | tf_op jit(solution)/shard_map/ppermute | solution.py:220
  50.1 12.6 %shard_map.83 = (f32[12,1,512]{2,1,0:T(1,128)}, f32[12,1,512]{2,1,0:T(1,128)}, f32[768,512]{1,0:T(8,128)}) custom-call(s32[10]{0:T(128)} %get-tuple-element.43.info_ref, bf16[512,768]{1,0:T(8,128)(2,1)} %bitcast.37, bf16[8,128,768]{2,1,0:T(8,128)(2,1)} %bitcast.13.k_ref.v_ref, bf16[8,128,768]{2,1,0:T(8,128)(2,1)} %bitcast.13.k_ref.v_ref, ...), custom_call_target="tpu_custom_call" | custom-call | flops 51539607552 | bytes 7864320 | tf_op jit(solution)/shard_map/pallas_call | solution.py:165
  62.7 11.5 %shard_map.84 = (f32[12,1,512]{2,1,0:T(1,128)}, f32[12,1,512]{2,1,0:T(1,128)}, f32[768,512]{1,0:T(8,128)}) custom-call(s32[10]{0:T(128)} %get-tuple-element.45.info_ref, bf16[512,768]{1,0:T(8,128)(2,1)} %bitcast.38, bf16[8,128,768]{2,1,0:T(8,128)(2,1)} %bitcast.12.k_ref.v_ref, bf16[8,128,768]{2,1,0:T(8,128)(2,1)} %bitcast.12.k_ref.v_ref, ...), custom_call_target="tpu_custom_call" | custom-call | flops 51539607552 | bytes 7864320 | tf_op jit(solution)/shard_map/pallas_call | solution.py:165
  74.2 10.6 %shard_map.85 = (f32[12,1,512]{2,1,0:T(1,128)}, f32[12,1,512]{2,1,0:T(1,128)}, f32[768,512]{1,0:T(8,128)}) custom-call(s32[10]{0:T(128)} %get-tuple-element.44.info_ref, bf16[512,768]{1,0:T(8,128)(2,1)} %bitcast.39, bf16[8,128,768]{2,1,0:T(8,128)(2,1)} %bitcast.10.k_ref.v_ref, bf16[8,128,768]{2,1,0:T(8,128)(2,1)} %bitcast.10.k_ref.v_ref, ...), custom_call_target="tpu_custom_call" | custom-call | flops 51539607552 | bytes 7864320 | tf_op jit(solution)/shard_map/pallas_call | solution.py:165
  84.8 0.0 collective-permute-done.3
  84.8 7.5 %shard_map.86 = (f32[12,1,512]{2,1,0:T(1,128)}, f32[12,1,512]{2,1,0:T(1,128)}, f32[768,512]{1,0:T(8,128)}) custom-call(s32[10]{0:T(128)} %get-tuple-element.42.info_ref, bf16[512,768]{1,0:T(8,128)(2,1)} %bitcast.40, bf16[8,128,768]{2,1,0:T(8,128)(2,1)} %bitcast.8.k_ref.v_ref, bf16[8,128,768]{2,1,0:T(8,128)(2,1)} %bitcast.8.k_ref.v_ref, ...), custom_call_target="tpu_custom_call" | custom-call | flops 51539607552 | bytes 7864320 | tf_op jit(solution)/shard_map/pallas_call | solution.py:165
  92.3 0.0 collective-permute-done.2
  92.3 8.4 %shard_map.87 = bf16[384,512]{1,0:T(8,128)(2,1)} custom-call(s32[10]{0:T(128)} %get-tuple-element.46.info_ref, bf16[512,768]{1,0:T(8,128)(2,1)} %bitcast.41, bf16[8,128,768]{2,1,0:T(8,128)(2,1)} %bitcast.6.k_ref.v_ref, bf16[8,128,768]{2,1,0:T(8,128)(2,1)} %bitcast.6.k_ref.v_ref, f32[12,1,512]{2,1,0:T(1,128)} %get-tuple-element.38.refs_0_, ...), custom_call_target="tpu_custom_call" | custom-call | flops 25769803776 | bytes 3932160 | tf_op jit(solution)/shard_map/pallas_call | solution.py:165
  100.7 0.0 copy-start.3
  100.7 8.5 %shard_map.88 = bf16[384,512]{1,0:T(8,128)(2,1)} custom-call(s32[10]{0:T(128)} %get-tuple-element.46.info_ref, bf16[512,768]{1,0:T(8,128)(2,1)} %bitcast.42, bf16[8,128,768]{2,1,0:T(8,128)(2,1)} %bitcast.6.k_ref.v_ref, bf16[8,128,768]{2,1,0:T(8,128)(2,1)} %bitcast.6.k_ref.v_ref, f32[12,1,512]{2,1,0:T(1,128)} %get-tuple-element.38.refs_0_, ...), custom_call_target="tpu_custom_call" | custom-call | flops 25769803776 | bytes 3932160 | tf_op jit(solution)/shard_map/pallas_call | solution.py:165
  109.2 0.0 copy-done.3
  109.2 0.3 collective-permute-start.4
  109.4 1.2 collective-permute-start.5
  110.6 0.0 copy-start
  110.6 1.8 %fusion.6 = f32[512,608]{0,1:T(8,128)S(1)} fusion(bf16[384,512]{1,0:T(8,128)(2,1)} %shard_map.88, bf16[1536,1216]{0,1:T(8,128)(2,1)} %param.15, s32[]{:T(128)S(6)} %select_n.44, s32[]{:T(128)S(6)} %select_n.50), kind=kOutput, calls=%fused_computation.8 | convolution fusion | flops 239075328 | bytes 2105352 | tf_op jit(solution)/shard_map/dot_general | solution.py:256
  112.5 0.0 copy-start.4
  112.5 1.7 %convolution_add_fusion = f32[512,608]{0,1:T(8,128)S(1)} fusion(f32[512,608]{0,1:T(8,128)S(1)} %fusion.6, bf16[384,512]{1,0:T(8,128)(2,1)S(1)} %copy-done.3, bf16[1536,1216]{0,1:T(8,128)(2,1)} %param.15, s32[]{:T(128)S(6)} %select_n.40, s32[]{:T(128)S(6)} %select_n.50), kind=kOutput, calls=%fused_computation | convolution fusion | flops 239386624 | bytes 3350536 | tf_op jit(solution)/shard_map/dot_general | solution.py:256
  114.2 0.0 copy-done
  114.2 0.0 copy-done.4
  114.2 0.6 fusion.13
  114.7 2.6 %collective-permute-done.4 = bf16[384,512]{1,0:T(8,128)(2,1)S(1)} collective-permute-done((bf16[384,512]{1,0:T(8,128)(2,1)S(1)}, bf16[384,512]{1,0:T(8,128)(2,1)S(1)}, u32[]{:S(2)}, u32[]{:S(2)}) %collective-permute-start.4) | collective-permute-done | bytes 393248 | tf_op jit(solution)/shard_map/ppermute | solution.py:19
  117.4 0.5 fusion.4
  117.9 7.9 %collective-permute-done.5 = bf16[384,512]{1,0:T(8,128)(2,1)S(1)} collective-permute-done((bf16[384,512]{1,0:T(8,128)(2,1)}, bf16[384,512]{1,0:T(8,128)(2,1)S(1)}, u32[]{:S(2)}, u32[]{:S(2)}) %collective-permute-start.5) | collective-permute-done | bytes 393248 | tf_op jit(solution)/shard_map/ppermute | solution.py:19
  125.8 0.6 add_convert_fusion.1
  126.4 3.4 %collective-permute-start.6 = (bf16[512,608]{0,1:T(8,128)(2,1)S(1)}, bf16[512,608]{0,1:T(8,128)(2,1)S(1)}, u32[]{:S(2)}, u32[]{:S(2)}) collective-permute-start(bf16[512,608]{0,1:T(8,128)(2,1)S(1)} %add_convert_fusion.1), channel_id=1, source_target_pairs={{0,1},{1,0},{2,3},{3,2},{4,5},{5,4},{6,7},{7,6},{8,9},{9,8},{10,11... | collective-permute-start | bytes 1867784 | tf_op jit(solution)/shard_map/ppermute | solution.py:19
  129.8 0.6 convolution_add_fusion.1
  130.3 0.6 fusion.11
  130.9 0.6 fusion.9
  131.4 0.0 collective-permute-done.6
  131.4 1.4 %add_convert_fusion = bf16[512,608]{0,1:T(8,128)(2,1)} fusion(bf16[512,608]{0,1:T(8,128)(2,1)S(1)} %collective-permute-done.6, f32[512,608]{0,1:T(8,128)S(1)} %fusion.9, f32[512,608]{0,1:T(8,128)S(1)} %convolution_add_fusion.1, f32[512,608]{0,1:T(8,128)S(1)} %fusion.11, f32[]{:T(128)S(6)} %sub.21, f32[]{:T(128)S(6)} %select_n.38), kind=kLoop, calls=%fused_computation.2 | loop fusion | flops 2179072 | bytes 4980744 | tf_op jit(solution)/shard_map/convert_element_type | solution.py:278
Async XLA Ops:
  0.0 2.2 %copy-start.5 = (bf16[1,512,768]{2,1,0:T(8,128)(2,1)S(1)}, bf16[1,512,768]{2,1,0:T(8,128)(2,1)}, u32[]{:S(2)}) copy-start(bf16[1,512,768]{2,1,0:T(8,128)(2,1)} %param.10) | copy-start | bytes 2359300
  0.0 9.6 %copy-start.1 = (bf16[1,4,333,768]{3,1,2,0:T(4,128)(2,1)S(1)}, bf16[1,4,333,768]{3,1,2,0:T(4,128)(2,1)}, u32[]{:S(2)}) copy-start(bf16[1,4,333,768]{3,1,2,0:T(4,128)(2,1)} %param.11) | copy-start | bytes 6137860
  3.2 37.5 %collective-permute-start = (bf16[2,512,768]{2,1,0:T(8,128)(2,1)}, bf16[2,512,768]{2,1,0:T(8,128)(2,1)}, u32[]{:S(2)}, u32[]{:S(2)}) collective-permute-start(bf16[2,512,768]{2,1,0:T(8,128)(2,1)} %constant_dynamic-update-slice_fusion), channel_id=1, source_target_pairs={{0,4},{4,8},{8,12},{1,5},{5,9},{9,13},{2,6},{6,10},{10,14},{3,7},{... | collective-permute-start | bytes 4718600 | tf_op jit(solution)/shard_map/ppermute | solution.py:219
  6.4 37.2 %collective-permute-start.1 = (bf16[2,512,768]{2,1,0:T(8,128)(2,1)}, bf16[2,512,768]{2,1,0:T(8,128)(2,1)}, u32[]{:S(2)}, u32[]{:S(2)}) collective-permute-start(bf16[2,512,768]{2,1,0:T(8,128)(2,1)} %constant_dynamic-update-slice_fusion), channel_id=1, source_target_pairs={{4,0},{8,4},{12,8},{5,1},{9,5},{13,9},{6,2},{10,6},{14,10},{7,3},{... | collective-permute-start | bytes 4718600 | tf_op jit(solution)/shard_map/ppermute | solution.py:220
  9.6 1.6 %copy-start.2 = (bf16[1,4,333,768]{3,1,2,0:T(4,128)(2,1)S(1)}, bf16[1,4,333,768]{3,1,2,0:T(4,128)(2,1)}, u32[]{:S(2)}) copy-start(bf16[1,4,333,768]{3,1,2,0:T(4,128)(2,1)} %param.12) | copy-start | bytes 6137860
  13.1 1.6 %copy-start.9 = (s32[4]{0:T(128)S(1)}, s32[4]{0:T(128)}, u32[]{:S(2)}) copy-start(s32[4]{0:T(128)} %param.14) | copy-start | bytes 52
  13.1 1.8 %copy-start.6 = (s32[1,4]{1,0:T(1,128)S(1)}, s32[1,4]{1,0:T(1,128)}, u32[]{:S(2)}) copy-start(s32[1,4]{1,0:T(1,128)} %param.13) | copy-start | bytes 52
  14.8 19.4 %copy-start.8 = (s32[4,1]{0,1:T(1,128)}, s32[4,1]{0,1:T(1,128)S(1)}, u32[]{:S(2)}) copy-start(s32[4,1]{0,1:T(1,128)S(1)} %reduce-window.9) | copy-start | bytes 52
  15.5 18.7 %copy-start.7 = (s32[1,4]{1,0:T(1,128)S(1)}, s32[1,4]{1,0:T(1,128)}, u32[]{:S(2)}) copy-start(s32[1,4]{1,0:T(1,128)} %param.13) | copy-start | bytes 52
  43.5 41.3 %collective-permute-start.3 = (bf16[2,512,768]{2,1,0:T(8,128)(2,1)}, bf16[2,512,768]{2,1,0:T(8,128)(2,1)}, u32[]{:S(2)}, u32[]{:S(2)}) collective-permute-start(bf16[2,512,768]{2,1,0:T(8,128)(2,1)} %collective-permute-done), channel_id=1, source_target_pairs={{0,4},{4,8},{8,12},{1,5},{5,9},{9,13},{2,6},{6,10},{10,14},{3,7},{... | collective-permute-start | bytes 4718600 | tf_op jit(solution)/shard_map/ppermute | solution.py:219
  46.7 45.5 %collective-permute-start.2 = (bf16[2,512,768]{2,1,0:T(8,128)(2,1)}, bf16[2,512,768]{2,1,0:T(8,128)(2,1)}, u32[]{:S(2)}, u32[]{:S(2)}) collective-permute-start(bf16[2,512,768]{2,1,0:T(8,128)(2,1)} %collective-permute-done.1), channel_id=1, source_target_pairs={{4,0},{8,4},{12,8},{5,1},{9,5},{13,9},{6,2},{10,6},{14,10},{7,3},{... | collective-permute-start | bytes 4718600 | tf_op jit(solution)/shard_map/ppermute | solution.py:220
  100.7 8.5 %copy-start.3 = (bf16[384,512]{1,0:T(8,128)(2,1)S(1)}, bf16[384,512]{1,0:T(8,128)(2,1)}, u32[]{:S(2)}) copy-start(bf16[384,512]{1,0:T(8,128)(2,1)} %shard_map.87) | copy-start | bytes 1179652
  109.2 8.2 %collective-permute-start.4 = (bf16[384,512]{1,0:T(8,128)(2,1)S(1)}, bf16[384,512]{1,0:T(8,128)(2,1)S(1)}, u32[]{:S(2)}, u32[]{:S(2)}) collective-permute-start(bf16[384,512]{1,0:T(8,128)(2,1)S(1)} %copy-done.3), channel_id=1, source_target_pairs={{0,2},{2,0},{1,3},{3,1},{4,6},{6,4},{5,7},{7,5},{8,10},{10,8},{9,1... | collective-permute-start | bytes 1179656 | tf_op jit(solution)/shard_map/ppermute | solution.py:19
  109.4 16.4 %collective-permute-start.5 = (bf16[384,512]{1,0:T(8,128)(2,1)}, bf16[384,512]{1,0:T(8,128)(2,1)S(1)}, u32[]{:S(2)}, u32[]{:S(2)}) collective-permute-start(bf16[384,512]{1,0:T(8,128)(2,1)} %shard_map.88), channel_id=1, source_target_pairs={{0,2},{2,0},{1,3},{3,1},{4,6},{6,4},{5,7},{7,5},{8,10},{10,8},{9,1... | collective-permute-start | bytes 1179656 | tf_op jit(solution)/shard_map/ppermute | solution.py:19
  110.6 3.5 %copy-start = (bf16[1536,1216]{0,1:T(8,128)(2,1)S(1)}, bf16[1536,1216]{0,1:T(8,128)(2,1)}, u32[]{:S(2)}) copy-start(bf16[1536,1216]{0,1:T(8,128)(2,1)} %param.15) | copy-start | bytes 11206660
  112.5 1.7 %copy-start.4 = (bf16[384,512]{1,0:T(8,128)(2,1)S(1)}, bf16[384,512]{1,0:T(8,128)(2,1)}, u32[]{:S(2)}) copy-start(bf16[384,512]{1,0:T(8,128)(2,1)} %shard_map.88) | copy-start | bytes 1179652
  126.4 5.1 %collective-permute-start.6 = (bf16[512,608]{0,1:T(8,128)(2,1)S(1)}, bf16[512,608]{0,1:T(8,128)(2,1)S(1)}, u32[]{:S(2)}, u32[]{:S(2)}) collective-permute-start(bf16[512,608]{0,1:T(8,128)(2,1)S(1)} %add_convert_fusion.1), channel_id=1, source_target_pairs={{0,1},{1,0},{2,3},{3,2},{4,5},{5,4},{6,7},{7,6},{8,9},{9,8},{10,11... | collective-permute-start | bytes 1867784 | tf_op jit(solution)/shard_map/ppermute | solution.py:19
